TPU v7x, 512 devices: a whole 4x4x16 slice. The times are simulated.
512 devices in a mesh: seq: 32 (over z_lo, y), tensor: 8 (over z_hi, x), enc: 2 (over core).
Axes of the slice: x: 4, y: 4, z: 16 (z_hi: 2, z_lo: 8; z = z_hi * 8 + z_lo), core: 2. Of those that a mesh axis runs over, the one named last changes fastest.
Arguments:
- neighbour_rows: bfloat16 [32768, 1024], P('seq'), may hold values from -17 to 17
- norm_gain: float32 [1024], replicated, may hold values from 0.1 to 1.9
- up_weight: bfloat16 [1024, 4096], P(None, ('tensor', 'enc')), may hold values from -0.1875 to 0.1875
- down_weight: bfloat16 [4096, 1024], P(('tensor', 'enc')), may hold values from -0.09375 to 0.09375
- final_gain: float32 [1024], replicated, may hold values from 0.1 to 1.9
- key_weight: bfloat16 [1024, 4096], P(None, ('tensor', 'enc')), may hold values from -0.1875 to 0.1875
- value_weight: bfloat16 [1024, 4096], P(None, ('tensor', 'enc')), may hold values from -0.1875 to 0.1875
- queries: bfloat16 [32768, 4096], P('seq', ('tensor', 'enc')), may hold values from -170 to 170
- block_lists: int32 [512, 2], P('seq'), may hold values from 0 to 255, as said below
- live_counts: int32 [512], P('seq'), may hold values from 1 to 2
Outputs:
- attended: bfloat16 [32768, 4096], P('seq', ('tensor', 'enc'))
Inputs may be any that keep to these rules, and one draw needn't show every extreme that they name: `block_lists`: block b of the pool lies on the device of index b // 8 along seq. The two entries of a span name blocks of two different devices. Among all list entries of one device's spans (those beyond a span's count included) at most 1 name blocks of any one device, and in every draw some device's entries reach 1 for some device.
All inputs are finite; a program needn't handle non-finite values.
Results may differ from a plain program's by a relative error of at most 0.019.
The roundings to bfloat16 on the way count: a program that leaves them out, or rounds other values in their place, can miss the bound.
Values may be sent and summed in bfloat16 or wider, within the bound.
No kernel may reach another device: no remote copies, remote signals or barrier semaphores. Data moves between devices by JAX's collectives and lax.ppermute only.
A program may use at most 64 MiB of HBM per device.

v0:
```python
import math
import jax
import jax.numpy as jnp
from jax import lax
from jax.sharding import PartitionSpec as P

DH = 128
NB = 128
CL = 64
KMAX = 2
TAG = 128


def rms_scale(rows, gain):
    mean_square = jnp.mean(rows * rows, axis=-1, keepdims=True)
    return rows * lax.rsqrt(mean_square + 1e-06) * gain


def need_ranks(owners):
    need_count = owners.shape[-1]
    order_index = jnp.arange(need_count)
    same_owner = owners[..., :, None] == owners[..., None, :]
    earlier = order_index[None, :] < order_index[:, None]
    return jnp.sum(jnp.logical_and(same_owner, earlier), axis=-1)


def shards(
    neighbour_rows,
    norm_gain,
    up_weight,
    down_weight,
    final_gain,
    key_weight,
    value_weight,
    queries,
    block_lists,
    live_counts,
):
    block_rows = neighbour_rows.shape[0]
    blocks = block_rows // NB
    head_width = key_weight.shape[1]
    heads_local = head_width // DH
    seq_count = lax.axis_size("seq")
    span_count = live_counts.shape[0]
    need_count = span_count * KMAX
    capacity = (need_count + seq_count - 1) // seq_count
    slots = seq_count * capacity
    q_width = CL * head_width
    flat_lists = block_lists.reshape(need_count)
    owners = flat_lists // blocks
    rank_order = need_ranks(owners)
    slot_index = owners * capacity + rank_order
    slot_range = jnp.arange(slots)
    slot_match = slot_index[None, :] == slot_range[:, None]
    entry_of_slot = jnp.sum(jnp.where(slot_match, jnp.arange(need_count)[None, :], 0), axis=1)
    filled = jnp.any(slot_match, axis=1)
    span_of_slot = entry_of_slot // KMAX
    block_of_slot = jnp.where(filled, flat_lists[entry_of_slot] % blocks, 0)
    span_queries = queries.reshape(span_count, q_width)
    sent_queries = jnp.take(span_queries, span_of_slot, axis=0)
    sent_queries = jnp.where(filled[:, None], sent_queries, jnp.zeros((), jnp.bfloat16))
    tag = jnp.broadcast_to(block_of_slot.astype(jnp.bfloat16)[:, None], (slots, TAG))
    outgoing = jnp.concatenate([sent_queries, tag], axis=1)
    incoming = lax.all_to_all(outgoing, "seq", split_axis=0, concat_axis=0, tiled=True)
    widened = neighbour_rows.astype(jnp.float32)
    normed = rms_scale(widened, norm_gain).astype(jnp.bfloat16)
    hidden = jax.nn.gelu(jnp.dot(normed, up_weight, preferred_element_type=jnp.float32)).astype(
        jnp.bfloat16
    )
    partial_sum = jnp.dot(hidden, down_weight, preferred_element_type=jnp.float32)
    reduced = lax.psum_scatter(partial_sum, ("tensor", "enc"), scatter_dimension=0, tiled=True)
    piece_rows = reduced.shape[0]
    piece = lax.axis_index("tensor") * lax.axis_size("enc") + lax.axis_index("enc")
    own_rows = lax.dynamic_slice_in_dim(neighbour_rows, piece * piece_rows, piece_rows, axis=0)
    encoded = own_rows.astype(jnp.float32) + reduced
    final_piece = rms_scale(encoded, final_gain).astype(jnp.bfloat16)
    final_rows = lax.all_gather(final_piece, ("tensor", "enc"), axis=0, tiled=True)
    key_part = jnp.dot(final_rows, key_weight, preferred_element_type=jnp.float32).astype(
        jnp.bfloat16
    )
    value_part = jnp.dot(final_rows, value_weight, preferred_element_type=jnp.float32).astype(
        jnp.bfloat16
    )
    key_blocks = key_part.reshape(blocks, NB, heads_local, DH)
    value_blocks = value_part.reshape(blocks, NB, heads_local, DH)
    in_queries = incoming[:, :q_width].reshape(slots, CL, heads_local, DH)
    in_block = incoming[:, q_width].astype(jnp.int32)
    in_block = jnp.clip(in_block, 0, blocks - 1)
    key_tiles = jnp.take(key_blocks, in_block, axis=0)
    value_tiles = jnp.take(value_blocks, in_block, axis=0)
    scores = jnp.einsum(
        "sqhd,skhd->shqk", in_queries, key_tiles, preferred_element_type=jnp.float32
    ) / math.sqrt(DH)
    local_max = jnp.max(scores, axis=-1, keepdims=True)
    weights = jnp.exp(scores - local_max)
    local_total = jnp.sum(weights, axis=-1)
    summed = jnp.einsum(
        "shqk,skhd->sqhd",
        weights.astype(jnp.bfloat16),
        value_tiles,
        preferred_element_type=jnp.float32,
    )
    stats = jnp.concatenate(
        [local_max[..., 0].reshape(slots, -1), local_total.reshape(slots, -1)], axis=1
    )
    reply = jnp.concatenate([summed.reshape(slots, q_width), stats], axis=1)
    returned = lax.all_to_all(reply, "seq", split_axis=0, concat_axis=0, tiled=True)
    stat_width = heads_local * CL
    picked = jnp.take(returned, slot_index, axis=0).reshape(span_count, KMAX, -1)
    part_sum = picked[..., :q_width].reshape(span_count, KMAX, CL, heads_local, DH)
    part_max = picked[..., q_width : q_width + stat_width].reshape(
        span_count, KMAX, heads_local, CL
    )
    part_total = picked[..., q_width + stat_width :].reshape(span_count, KMAX, heads_local, CL)
    live_mask = (jnp.arange(KMAX)[None, :] < live_counts[:, None])[:, :, None, None]
    part_max = jnp.where(live_mask, part_max, -jnp.inf)
    highest = jnp.max(part_max, axis=1, keepdims=True)
    scale = jnp.where(live_mask, jnp.exp(part_max - highest), 0.0)
    row_total = jnp.sum(scale * part_total, axis=1)
    scale_rows = jnp.transpose(scale, (0, 1, 3, 2))[..., None]
    combined = jnp.sum(jnp.where(scale_rows > 0, scale_rows * part_sum, 0.0), axis=1)
    result = combined / jnp.transpose(row_total, (0, 2, 1))[..., None]
    return result.reshape(span_count * CL, head_width).astype(jnp.bfloat16)


def solution(mesh):
    placed = (
        P("seq", None),
        P(),
        P(None, ("tensor", "enc")),
        P(("tensor", "enc"), None),
        P(),
        P(None, ("tensor", "enc")),
        P(None, ("tensor", "enc")),
        P("seq", ("tensor", "enc")),
        P("seq", None),
        P("seq"),
    )
    return jax.shard_map(
        shards, mesh=mesh, in_specs=placed, out_specs=P("seq", ("tensor", "enc")), check_vma=False
    )
```

profile of v0, /device:TPU:1, one launch (start us, length us, event | category | flops | bytes accessed | tf_op | source)
XLA Modules:
  0.0 442.7 jit_solution(8348694677223937590)
XLA Ops:
  6.5 2.2 fusion
  8.9 5.3 %fusion.33 = f32[1024,1024]{1,0:T(8,128)} fusion(bf16[256,1024]{1,0:T(8,128)(2,1)S(1)} %copy-done, bf16[1024,256]{1,0:T(8,128)(2,1)} %param.14, bf16[1024,1024]{1,0:T(8,128)(2,1)S(1)} %copy-done.2, f32[1024]{0:T(1024)S(1)} %copy-done.8, f32[1024]{0:T(1024)S(1)} %add_rsqrt_fusion), kind=kOutput, calls=%fused_computation.42 | convolution fusion | flops 1080295424 | bytes 7348224 | tf_op jit(solution)/shard_map/dot_general | solution.py:70
  18.6 1.4 reduce.3
  20.0 1.6 reshape.393
  21.7 16.2 %all-to-all-start = ((bf16[32,2,8256]{2,1,0:T(2,128)(2,1)}), bf16[32,2,8256]{2,1,0:T(2,128)(2,1)}, u32[]{:S(2)}, u32[]{:S(2)}) async-start(bf16[32,2,8256]{2,1,0:T(2,128)(2,1)} %reshape.393), calls=%async_computation.1 | async-start | bytes 2129920 | tf_op jit(solution)/shard_map/all_to_all | solution.py:64
  38.1 145.8 %reduce-scatter.2.cloned.1.call-done = f32[64,1024]{1,0:T(8,128)} async-done(((f32[1024,1024]{1,0:T(8,128)}), f32[64,1024]{1,0:T(8,128)}) %reduce-scatter.2.cloned.1.call-update) | async-done | bytes 262160 | tf_op jit(solution)/shard_map/reduce_scatter | solution.py:71
  185.0 1.7 multiply_convert_fusion
  186.8 4.4 %reshape.394 = bf16[32,1,16512]{2,1,0:T(2,128)(2,1)S(1)} reshape(bf16[32,2,8256]{2,1,0:T(2,128)(2,1)} %all-to-all-done) | data formatting | bytes 2113536
  191.2 5.3 %copy.112 = bf16[32,1,16512]{0,2,1:T(8,128)(2,1)} copy(bf16[32,1,16512]{2,1,0:T(2,128)(2,1)S(1)} %reshape.394) | data formatting | bytes 2113536 | tf_op jit(solution)/shard_map/all_to_all | solution.py:64
  196.5 3.8 slice.30
  200.3 4.9 %copy.116 = bf16[32,64,2,128]{3,1,2,0:T(8,128)(2,1)} copy(bf16[32,64,2,128]{0,3,2,1:T(8,128)(2,1)} %bitcast.63) | data formatting | bytes 2097152 | tf_op jit(solution)/shard_map/reshape | solution.py:86
  205.9 65.9 %all-gather.2.cloned.1.call-done = bf16[1024,1024]{1,0:T(8,128)(2,1)} async-done(((bf16[64,1024]{1,0:T(8,128)(2,1)}), bf16[1024,1024]{1,0:T(8,128)(2,1)}) %all-gather.2.cloned.1.call-update) | async-done | bytes 2097168 | tf_op jit(solution)/shard_map/all_gather | solution.py:77
  271.8 2.3 convolution_convert_fusion.1
  275.1 2.3 convolution_convert_fusion
  277.7 2.2 gather_fusion.4
  279.9 3.6 multiply_reduce_fusion
  285.0 2.2 gather_fusion.3
  287.2 2.4 fusion.17
  289.5 3.0 copy.117
  292.5 2.9 reshape.343
  295.6 3.5 copy.118
  299.1 5.3 %all-to-all-start.1 = ((f32[32,1,16640]{2,1,0:T(1,128)}), f32[32,1,16640]{2,1,0:T(1,128)}, u32[]{:S(2)}, u32[]{:S(2)}) async-start(f32[32,1,16640]{2,1,0:T(1,128)} %copy.118), calls=%async_computation.2 | async-start | bytes 4259840 | tf_op jit(solution)/shard_map/all_to_all | solution.py:107
  304.8 96.1 %all-to-all-done.1 = f32[32,1,16640]{2,1,0:T(1,128)} async-done(((f32[32,1,16640]{2,1,0:T(1,128)}), f32[32,1,16640]{2,1,0:T(1,128)}, u32[]{:S(2)}, u32[]{:S(2)}) %all-to-all-start.1) | async-done | bytes 2129952 | tf_op jit(solution)/shard_map/all_to_all | solution.py:107
  400.9 1.7 copy.143
  402.7 2.5 gather_fusion.2
  405.2 3.5 gather.19
  408.7 1.8 copy_select_fusion
  411.8 4.3 broadcast_in_dim.130
  416.1 3.0 broadcast_in_dim.131
  420.5 4.8 %mul.99 = f32[16,2,64,2,128]{4,3,2,0,1:T(2,128)} broadcast(f32[16,2,64,2]{3,2,0,1:T(8,128)} %copy.124), dimensions={0,1,2,3} | broadcast | bytes 2113536 | tf_op jit(solution)/shard_map/mul | solution.py:121
  425.3 3.9 mul.100
  429.2 3.0 fusion.6
  (76 shorter events, 16.0 us)
Async XLA Ops:
  6.5 2.2 copy-start
  6.5 2.4 copy-start.2
  6.5 2.4 copy-start.8
  6.5 177.3 %reduce-scatter.2.cloned.1.call-start = ((), (), s32[]{:S(2)}) async-start(), calls=%async_computation.3 | async-start | bytes 4456448 | tf_op jit(solution)/shard_map/reduce_scatter | solution.py:71
  14.2 0.7 copy-start.5
  14.2 1.9 copy-start.3
  20.0 165.0 %copy-start.4 = (f32[1024]{0:T(1024)S(1)}, f32[1024]{0:T(1024)}, u32[]{:S(2)}) copy-start(f32[1024]{0:T(1024)} %param.16) | copy-start | bytes 12292
  21.7 165.1 %all-to-all-start = ((bf16[32,2,8256]{2,1,0:T(2,128)(2,1)}), bf16[32,2,8256]{2,1,0:T(2,128)(2,1)}, u32[]{:S(2)}, u32[]{:S(2)}) async-start(bf16[32,2,8256]{2,1,0:T(2,128)(2,1)} %reshape.393), calls=%async_computation.1 | async-start | bytes 2129920 | tf_op jit(solution)/shard_map/all_to_all | solution.py:64
  37.9 233.9 %all-gather.2.cloned.1.call-start = ((), (), s32[]{:S(2)}) async-start(), calls=%async_computation.4 | async-start | bytes 2228224 | tf_op jit(solution)/shard_map/all_gather | solution.py:77
  200.3 71.5 %copy-start.6 = (bf16[1024,256]{1,0:T(8,128)(2,1)S(1)}, bf16[1024,256]{1,0:T(8,128)(2,1)}, u32[]{:S(2)}) copy-start(bf16[1024,256]{1,0:T(8,128)(2,1)} %param.18) | copy-start | bytes 1572868
  274.1 1.0 copy-start.7
  299.1 5.6 %copy-start.9 = (s32[16]{0:T(128)S(1)}, s32[16]{0:T(128)}, u32[]{:S(2)}) copy-start(s32[16]{0:T(128)} %param.21) | copy-start | bytes 196
  299.1 101.8 %all-to-all-start.1 = ((f32[32,1,16640]{2,1,0:T(1,128)}), f32[32,1,16640]{2,1,0:T(1,128)}, u32[]{:S(2)}, u32[]{:S(2)}) async-start(f32[32,1,16640]{2,1,0:T(1,128)} %copy.118), calls=%async_computation.2 | async-start | bytes 4259840 | tf_op jit(solution)/shard_map/all_to_all | solution.py:107
  432.2 3.6 copy-start.1
Sparse Core Ops, SparseCore 0:
  14.3 169.5 reduce-scatter.1
  187.2 84.5 all-gather.1
where the time goes:
time: 444 us; the launch traced here: 443 us
  waiting for transfers between devices  308 us (69%)
  local copies, waits for them, and re-layouts  68 us (15%)
  starting transfers between devices  21.7 us (5%)
  matrix products  15.8 us (4%)
  other arithmetic  15.6 us (4%)
  between operations  13.8 us (3%)
    reduce_scatter x1, waiting for transfers between devices, shards(): lax.psum_scatter(partial_sum, ('tensor', 'enc'), scatter_dimension=0, til...  146 us
    all_to_all x1, waiting for transfers between devices, shards(): lax.all_to_all(reply, 'seq', split_axis=0, concat_axis=0, tiled=True)  96.1 us
    all_gather x1, waiting for transfers between devices, shards(): lax.all_gather(final_piece, ('tensor', 'enc'), axis=0, tiled=True)  65.9 us
    all_to_all x1, starting transfers between devices, shards(): lax.all_to_all(outgoing, 'seq', split_axis=0, concat_axis=0, tiled=True)  16.2 us
    unnamed x24, local copies, waits for them, and re-layouts  9.49 us
  transfers between devices with their start and end apart: 4, of which 3 were waited for; matrix products, arithmetic and copies ran while one was open for 7% of the time, Pallas kernels for 0%

commit v1 on v0

--- a/solution.py
+++ b/solution.py
@@ -74,7 +74,10 @@
     own_rows = lax.dynamic_slice_in_dim(neighbour_rows, piece * piece_rows, piece_rows, axis=0)
     encoded = own_rows.astype(jnp.float32) + reduced
     final_piece = rms_scale(encoded, final_gain).astype(jnp.bfloat16)
-    final_rows = lax.all_gather(final_piece, ("tensor", "enc"), axis=0, tiled=True)
+    size = lax.axis_size(("tensor", "enc"))
+    pieces = jnp.stack([final_piece for _ in range(size)])
+    pieces = lax.all_to_all(pieces, ("tensor", "enc"), split_axis=0, concat_axis=0)
+    final_rows = jnp.concatenate(pieces, axis=0)
     key_part = jnp.dot(final_rows, key_weight, preferred_element_type=jnp.float32).astype(
         jnp.bfloat16
     )

time: 444 us -> 474 us (1.068)
  starting transfers between devices: 21.7 us -> 86.3 us
  waiting for transfers between devices: 308 us -> 271 us
    all_gather x1 -> x0, waiting for transfers between devices: 65.9 us -> none  [shards(): lax.all_gather(final_piece, ('tensor', 'enc'), axis=0, tiled=True)]
    all_to_all x1, starting transfers between devices: 5.3 us -> 63.8 us  [shards(): lax.all_to_all(reply, 'seq', split_axis=0, concat_axis=0, tiled=True)]
    all_to_all x0 -> x1, waiting for transfers between devices: none -> 28.9 us  [shards(): lax.all_to_all(pieces, ('tensor', 'enc'), split_axis=0, concat_axis=0)]
    all_to_all x0 -> x1, starting transfers between devices: none -> 6.41 us  [shards(): lax.all_to_all(pieces, ('tensor', 'enc'), split_axis=0, concat_axis=0)]
    unnamed x24 -> x26, local copies, waits for them, and re-layouts: 9.49 us -> 8.7 us
  transfers between devices with their start and end apart: 4 -> 4, of which waited for: 3 -> 3; matrix products, arithmetic and copies ran while one was open for 7% -> 6% of each run, Pallas kernels for 0% -> 0%
where the time goes in v1:
time: 474 us; the launch traced here: 471 us
  waiting for transfers between devices  271 us (57%)
  starting transfers between devices  86.3 us (18%)
  local copies, waits for them, and re-layouts  68.8 us (15%)
  matrix products  15.9 us (3%)
  other arithmetic  14.9 us (3%)
  between operations  13.8 us (3%)
    reduce_scatter x1, waiting for transfers between devices, shards(): lax.psum_scatter(partial_sum, ('tensor', 'enc'), scatter_dimension=0, til...  146 us
    all_to_all x1, waiting for transfers between devices, shards(): lax.all_to_all(reply, 'seq', split_axis=0, concat_axis=0, tiled=True)  96 us
    all_to_all x1, starting transfers between devices, shards(): lax.all_to_all(reply, 'seq', split_axis=0, concat_axis=0, tiled=True)  63.8 us
    all_to_all x1, waiting for transfers between devices, shards(): lax.all_to_all(pieces, ('tensor', 'enc'), split_axis=0, concat_axis=0)  28.9 us
    all_to_all x1, starting transfers between devices, shards(): lax.all_to_all(outgoing, 'seq', split_axis=0, concat_axis=0, tiled=True)  16.1 us
  transfers between devices with their start and end apart: 4, of which 3 were waited for; matrix products, arithmetic and copies ran while one was open for 6% of the time, Pallas kernels for 0%

profile of v1, /device:TPU:1, one launch (start us, length us, event | category | flops | bytes accessed | tf_op | source)
XLA Modules:
  0.0 470.7 jit_solution(362452721265821700)
XLA Ops:
  6.5 2.2 fusion
  8.9 5.3 %fusion.33 = f32[1024,1024]{1,0:T(8,128)} fusion(bf16[256,1024]{1,0:T(8,128)(2,1)S(1)} %copy-done, bf16[1024,256]{1,0:T(8,128)(2,1)} %param.14, bf16[1024,1024]{1,0:T(8,128)(2,1)S(1)} %copy-done.3, f32[1024]{0:T(1024)S(1)} %copy-done.9, f32[1024]{0:T(1024)S(1)} %add_rsqrt_fusion), kind=kOutput, calls=%fused_computation.42 | convolution fusion | flops 1080295424 | bytes 7348224 | tf_op jit(solution)/shard_map/dot_general | solution.py:70
  20.1 1.6 reshape.399
  21.7 16.1 %all-to-all-start.1 = ((bf16[32,2,8256]{2,1,0:T(2,128)(2,1)}), bf16[32,2,8256]{2,1,0:T(2,128)(2,1)S(1)}, u32[]{:S(2)}, u32[]{:S(2)}) async-start(bf16[32,2,8256]{2,1,0:T(2,128)(2,1)} %reshape.399), calls=%async_computation.2 | async-start | bytes 2129920 | tf_op jit(solution)/shard_map/all_to_all | solution.py:64
  37.8 146.1 %reduce-scatter.2.cloned.1.call-done = f32[64,1024]{1,0:T(8,128)} async-done(((f32[1024,1024]{1,0:T(8,128)}), f32[64,1024]{1,0:T(8,128)}) %reduce-scatter.2.cloned.1.call-update) | async-done | bytes 262160 | tf_op jit(solution)/shard_map/reduce_scatter | solution.py:71
  186.2 1.7 stack.2
  187.8 6.4 %all-to-all-start = ((bf16[16,64,1024]{2,1,0:T(8,128)(2,1)}), bf16[16,64,1024]{2,1,0:T(8,128)(2,1)}, u32[]{:S(2)}, u32[]{:S(2)}) async-start(bf16[16,64,1024]{2,1,0:T(8,128)(2,1)} %stack.2), calls=%async_computation.1 | async-start | bytes 4194304 | tf_op jit(solution)/shard_map/all_to_all | solution.py:79
  194.2 4.4 reshape.400
  198.7 5.3 %copy.112 = bf16[32,1,16512]{0,2,1:T(8,128)(2,1)} copy(bf16[32,1,16512]{2,1,0:T(2,128)(2,1)S(1)} %reshape.400) | data formatting | bytes 2113536 | tf_op jit(solution)/shard_map/all_to_all | solution.py:64
  203.9 3.7 slice.30
  207.6 5.0 %copy.116 = bf16[32,64,2,128]{3,1,2,0:T(8,128)(2,1)} copy(bf16[32,64,2,128]{0,3,2,1:T(8,128)(2,1)} %bitcast.64) | data formatting | bytes 2097152 | tf_op jit(solution)/shard_map/reshape | solution.py:89
  213.3 28.9 %all-to-all-done = bf16[16,64,1024]{2,1,0:T(8,128)(2,1)} async-done(((bf16[16,64,1024]{2,1,0:T(8,128)(2,1)}), bf16[16,64,1024]{2,1,0:T(8,128)(2,1)}, u32[]{:S(2)}, u32[]{:S(2)}) %all-to-all-start) | async-done | bytes 2097184 | tf_op jit(solution)/shard_map/all_to_all | solution.py:79
  242.2 2.4 convolution_convert_fusion
  244.6 2.3 convolution_convert_fusion.1
  247.4 2.2 gather_fusion.4
  249.6 3.6 multiply_reduce_fusion
  254.7 2.2 gather_fusion.3
  256.9 2.4 fusion.17
  259.2 3.0 copy.117
  262.2 2.9 reshape.349
  265.3 3.5 copy.118
  268.8 63.8 %all-to-all-start.2 = ((f32[32,1,16640]{2,1,0:T(1,128)}), f32[32,1,16640]{2,1,0:T(1,128)}, u32[]{:S(2)}, u32[]{:S(2)}) async-start(f32[32,1,16640]{2,1,0:T(1,128)} %copy.118), calls=%async_computation.3 | async-start | bytes 4259840 | tf_op jit(solution)/shard_map/all_to_all | solution.py:110
  333.0 96.0 %all-to-all-done.2 = f32[32,1,16640]{2,1,0:T(1,128)} async-done(((f32[32,1,16640]{2,1,0:T(1,128)}), f32[32,1,16640]{2,1,0:T(1,128)}, u32[]{:S(2)}, u32[]{:S(2)}) %all-to-all-start.2) | async-done | bytes 2129952 | tf_op jit(solution)/shard_map/all_to_all | solution.py:110
  429.0 1.7 copy.143
  430.7 2.5 gather_fusion.2
  433.2 3.5 gather.19
  436.7 1.8 copy_select_fusion
  439.8 4.3 broadcast_in_dim.130
  444.1 3.0 broadcast_in_dim.131
  448.5 4.8 %mul.99 = f32[16,2,64,2,128]{4,3,2,0,1:T(2,128)} broadcast(f32[16,2,64,2]{3,2,0,1:T(8,128)} %copy.124), dimensions={0,1,2,3} | broadcast | bytes 2113536 | tf_op jit(solution)/shard_map/mul | solution.py:124
  453.3 3.9 mul.100
  457.2 3.0 fusion.6
  (78 shorter events, 17.5 us)
Async XLA Ops:
  6.5 2.2 copy-start
  6.5 2.4 copy-start.3
  6.5 2.4 copy-start.9
  6.5 177.4 %reduce-scatter.2.cloned.1.call-start = ((), (), s32[]{:S(2)}) async-start(), calls=%async_computation.4 | async-start | bytes 4456448 | tf_op jit(solution)/shard_map/reduce_scatter | solution.py:71
  14.2 0.7 copy-start.6
  14.2 1.3 copy-start.4
  20.0 165.0 %copy-start.5 = (f32[1024]{0:T(1024)S(1)}, f32[1024]{0:T(1024)}, u32[]{:S(2)}) copy-start(f32[1024]{0:T(1024)} %param.16) | copy-start | bytes 12292
  21.7 164.5 %all-to-all-start.1 = ((bf16[32,2,8256]{2,1,0:T(2,128)(2,1)}), bf16[32,2,8256]{2,1,0:T(2,128)(2,1)S(1)}, u32[]{:S(2)}, u32[]{:S(2)}) async-start(bf16[32,2,8256]{2,1,0:T(2,128)(2,1)} %reshape.399), calls=%async_computation.2 | async-start | bytes 2129920 | tf_op jit(solution)/shard_map/all_to_all | solution.py:64
  186.2 1.7 copy-start.2
  187.8 54.4 %all-to-all-start = ((bf16[16,64,1024]{2,1,0:T(8,128)(2,1)}), bf16[16,64,1024]{2,1,0:T(8,128)(2,1)}, u32[]{:S(2)}, u32[]{:S(2)}) async-start(bf16[16,64,1024]{2,1,0:T(8,128)(2,1)} %stack.2), calls=%async_computation.1 | async-start | bytes 4194304 | tf_op jit(solution)/shard_map/all_to_all | solution.py:79
  207.6 34.6 %copy-start.7 = (bf16[1024,256]{1,0:T(8,128)(2,1)S(1)}, bf16[1024,256]{1,0:T(8,128)(2,1)}, u32[]{:S(2)}) copy-start(bf16[1024,256]{1,0:T(8,128)(2,1)} %param.17) | copy-start | bytes 1572868
  242.2 2.4 copy-start.8
  268.8 64.1 %copy-start.10 = (s32[16]{0:T(128)S(1)}, s32[16]{0:T(128)}, u32[]{:S(2)}) copy-start(s32[16]{0:T(128)} %param.21) | copy-start | bytes 196
  268.8 160.1 %all-to-all-start.2 = ((f32[32,1,16640]{2,1,0:T(1,128)}), f32[32,1,16640]{2,1,0:T(1,128)}, u32[]{:S(2)}, u32[]{:S(2)}) async-start(f32[32,1,16640]{2,1,0:T(1,128)} %copy.118), calls=%async_computation.3 | async-start | bytes 4259840 | tf_op jit(solution)/shard_map/all_to_all | solution.py:110
  460.2 3.6 copy-start.1
Sparse Core Ops, SparseCore 0:
  14.3 169.5 reduce-scatter.1
